TPU v7x, 32 devices: a whole 2x2x4 slice. The times are simulated.
32 devices in a mesh: layer: 4 (over x, core), row: 4 (over z), col: 2 (over y).
Axes of the slice: x: 2, y: 2, z: 4, core: 2. Of those that a mesh axis runs over, the one named last changes fastest.
Arguments:
- sources: float32 [8, 256, 1024], P('layer', 'row', 'col'), may hold values from -14 to 14
- conduct: float32 [8, 256, 1024], P('layer', 'row', 'col'), may hold values from 0.5 to 4
- via_cond: float32 [8, 256, 1024], P('layer', 'row', 'col'), may hold values from 0.5 to 4
- via_map: int32 [8, 256, 1024], P('layer', 'row', 'col'), may hold values 0 or 1
- pad_map: int32 [256, 1024], P('row', 'col'), may hold values 0 or 1
- port_tile: int32 [4, 512], replicated, may hold values from 0 to 1023
- pivots: float32 [4, 512, 512], P(None, 'col'), may hold values from -1 to 2, as said below
- coupling: float32 [3, 512, 512], P(None, 'col'), may hold values from -0.109375 to 0.109375
Outputs:
- drop: float32 [8, 256, 1024], P('layer', 'row', 'col')
- ports: float32 [4, 512], replicated
Inputs may be any that keep to these rules, and one draw needn't show every extreme that they name: `pivots`: each block is symmetric.
All inputs are finite; a program needn't handle non-finite values. No bound on the sum of `via_map` or of `pad_map` on one device may be relied on, other than what follows from the above.
Results may differ from a plain program's by a relative error of at most 0.00023.
Values sent between devices are 32-bit elements; how exact they have to be, the bound alone decides.
No kernel may reach another device: no remote copies, remote signals or barrier semaphores. Data moves between devices by JAX's collectives and lax.ppermute only.
A program may use at most 64 MiB of HBM per device.

v0:
```python
import jax
import jax.numpy as jnp
from jax import lax
from jax.sharding import PartitionSpec as P

TILE = 16
PANEL = 512
NPANEL = 4
DEG = 3
ITERS = 2
pad_gain = 8.0
bound_low = 0.1
bound_high = 1.9
restrict_scale = 0.25
prolong_scale = 0.5


def padded(cells, sides, width):
    for axis, dim in sides:
        count = lax.axis_size(axis)
        ends = count - 1
        head = lax.slice_in_dim(cells, 0, width, axis=dim)
        tail = lax.slice_in_dim(cells, cells.shape[dim] - width, cells.shape[dim], axis=dim)
        cells = jnp.concatenate(
            [
                lax.ppermute(tail, axis, [(i, (i + 1) % count) for i in range(ends)]),
                cells,
                lax.ppermute(head, axis, [((i + 1) % count, i) for i in range(ends)]),
            ],
            axis=dim,
        )
    return cells


def shifted(grown):
    return (
        grown[2:, 1:-1, 1:-1],
        grown[:-2, 1:-1, 1:-1],
        grown[1:-1, 2:, 1:-1],
        grown[1:-1, :-2, 1:-1],
        grown[1:-1, 1:-1, 2:],
        grown[1:-1, 1:-1, :-2],
    )


def layer_grow(stack):
    return padded(stack, (("layer", 1), ("row", 2), ("col", 3)), 1)


def apply_grid(field, weights, pad_term, grow):
    grown = grow(field[None])[0]
    result = pad_term * field
    for weight, other in zip(weights, shifted(grown)):
        result = result + weight * (field - other)
    return result


def smooth(resid, weights, pad_term, inverse, grow):
    theta = (bound_high + bound_low) / 2.0
    delta = (bound_high - bound_low) / 2.0
    sigma = theta / delta
    rho = 1.0 / sigma
    change = inverse * resid / theta
    total = change
    for sweep in range(DEG - 1):
        remain = resid - apply_grid(total, weights, pad_term, grow)
        rho_new = 1.0 / (2.0 * sigma - rho)
        change = rho_new * rho * change + 2.0 * rho_new / delta * inverse * remain
        total = total + change
        rho = rho_new
    return total


def shards(sources, conduct, via_cond, via_map, pad_map, port_tile, pivots, coupling):
    highest = lax.Precision.HIGHEST
    layer_count = lax.axis_size("layer")
    vertical = via_cond * via_map.astype(jnp.float32)
    block_rows = sources.shape[1]
    currents, plane_cond, plane_vert = (sources, conduct, vertical)
    row_start = lax.axis_index("row") * block_rows
    top_flag = (lax.axis_index("layer") == layer_count - 1).astype(jnp.float32)
    local_layers, grid_rows, grid_cols = currents.shape
    grown = layer_grow(jnp.stack((plane_cond, plane_vert)))
    near_plane = shifted(grown[0])
    near_vert = shifted(grown[1])
    weights = (
        jnp.sqrt(plane_vert * near_vert[0]),
        jnp.sqrt(plane_vert * near_vert[1]),
        jnp.sqrt(plane_cond * near_plane[2]),
        jnp.sqrt(plane_cond * near_plane[3]),
        jnp.sqrt(plane_cond * near_plane[4]),
        jnp.sqrt(plane_cond * near_plane[5]),
    )
    top_layer = pad_gain * pad_map.astype(jnp.float32) * top_flag
    pad_term = jnp.concatenate(
        (jnp.zeros((local_layers - 1, grid_rows, grid_cols), jnp.float32), top_layer[None]), 0
    )
    diagonal = pad_term
    for weight in weights:
        diagonal = diagonal + weight
    inverse = 1.0 / diagonal
    total_tile_cols = grid_cols * lax.axis_size("col") // TILE
    row_tiles = (row_start + jnp.arange(grid_rows, dtype=jnp.int32)) // TILE
    col_tiles = (lax.axis_index("col") * grid_cols + jnp.arange(grid_cols, dtype=jnp.int32)) // TILE
    flat_tiles = port_tile.reshape(-1)
    row_select = (flat_tiles[:, None] // total_tile_cols == row_tiles[None, :]).astype(jnp.float32)
    col_select = (flat_tiles[:, None] % total_tile_cols == col_tiles[None, :]).astype(jnp.float32)
    share = PANEL // lax.axis_size("col")
    start = lax.axis_index("col") * share
    drop = jnp.zeros((local_layers, grid_rows, grid_cols), jnp.float32)
    ports = jnp.zeros((NPANEL, PANEL), jnp.float32)
    for outer in range(ITERS):
        resid = currents - apply_grid(drop, weights, pad_term, layer_grow)
        plane = jnp.sum(resid, axis=0)
        row_sums = jnp.dot(row_select, plane, precision=highest)
        local_rhs = jnp.sum(row_sums * col_select, axis=1).reshape(NPANEL, PANEL)
        rhs = lax.psum(local_rhs, ("layer", "row", "col")) * (restrict_scale / TILE)
        full = rhs[0]
        forward = [full]
        for section in range(1, NPANEL):
            piece = lax.dynamic_slice_in_dim(rhs[section], start, share) - jnp.dot(
                coupling[section - 1], full, precision=highest
            )
            full = lax.all_gather(piece, "col", axis=0, tiled=True)
            forward.append(full)
        scaled = [
            jnp.dot(pivots[section], forward[section], precision=highest)
            for section in range(NPANEL)
        ]
        results = [None] * NPANEL
        for section in range(NPANEL - 1, -1, -1):
            placed = lax.dynamic_update_slice_in_dim(
                jnp.zeros((PANEL,), jnp.float32), scaled[section], start, 0
            )
            if section < NPANEL - 1:
                later_rows = lax.dynamic_slice_in_dim(results[section + 1], start, share)
                placed = placed - jnp.dot(later_rows, coupling[section], precision=highest)
            results[section] = lax.psum(placed, "col")
        ports = jnp.stack(results)
        weighted_rows = jnp.transpose(row_select) * ports.reshape(-1)[None, :]
        field = jnp.dot(weighted_rows, col_select, precision=highest) * prolong_scale
        lifted = jnp.broadcast_to(field[None], (local_layers, grid_rows, grid_cols))
        drop = drop + lifted + smooth(resid, weights, pad_term, inverse, layer_grow)
    return (drop, ports)


def solution(mesh):
    placed = (
        P("layer", "row", "col"),
        P("layer", "row", "col"),
        P("layer", "row", "col"),
        P("layer", "row", "col"),
        P("row", "col"),
        P(),
        P(None, "col", None),
        P(None, "col", None),
    )
    return jax.shard_map(
        shards,
        mesh=mesh,
        in_specs=placed,
        out_specs=(P("layer", "row", "col"), P()),
        check_vma=False,
    )
```

profile of v0, /device:TPU:2, one launch (start us, length us, event | category | flops | bytes accessed | tf_op | source)
XLA Modules:
  0.0 358.2 jit_solution(15294549524432224454)
XLA Ops:
  9.2 3.6 %collective-permute-start.1 = (f32[2,1,64,512]{3,2,1,0:T(8,128)S(1)}, f32[2,1,64,512]{3,2,1,0:T(8,128)S(1)}, u32[]{:S(2)}, u32[]{:S(2)}) collective-permute-start(f32[2,1,64,512]{3,2,1,0:T(8,128)S(1)} %get-tuple-element.41), channel_id=1, source_target_pairs={{8,0},{16,8},{24,16},{9,1},{17,9},{25,17},{10,2},{18,10},{26,18},{... | collective-permute-start | bytes 786440 | tf_op jit(solution)/shard_map/ppermute | solution.py:28
  17.9 4.5 %collective-permute-start.2 = (f32[2,4,1,512]{3,2,1,0:T(1,128)S(1)}, f32[2,4,1,512]{3,2,1,0:T(1,128)S(1)}, u32[]{:S(2)}, u32[]{:S(2)}) collective-permute-start(f32[2,4,1,512]{3,2,1,0:T(1,128)S(1)} %get-tuple-element.16), channel_id=1, source_target_pairs={{0,2},{2,4},{4,6},{1,3},{3,5},{5,7},{8,10},{10,12},{12,14},{9,11},... | collective-permute-start | bytes 49160 | tf_op jit(solution)/shard_map/ppermute | solution.py:26
  28.8 4.6 %collective-permute-start.4 = (f32[2,4,66,1]{3,2,1,0:T(8,128)S(1)}, f32[2,4,66,1]{3,2,1,0:T(8,128)S(1)}, u32[]{:S(2)}, u32[]{:S(2)}) collective-permute-start(f32[2,4,66,1]{3,2,1,0:T(8,128)S(1)} %get-tuple-element.14), channel_id=1, source_target_pairs={{0,1},{2,3},{4,5},{6,7},{8,9},{10,11},{12,13},{14,15},{16,17},{18,... | collective-permute-start | bytes 6344 | tf_op jit(solution)/shard_map/ppermute | solution.py:26
  37.6 4.4 %collective-permute-done.5 = f32[2,4,66,1]{3,2,1,0:T(8,128)S(1)} collective-permute-done((f32[2,4,66,1]{3,2,1,0:T(8,128)S(1)}, f32[2,4,66,1]{3,2,1,0:T(8,128)S(1)}, u32[]{:S(2)}, u32[]{:S(2)}) %collective-permute-start.5) | collective-permute-done | bytes 2144 | tf_op jit(solution)/shard_map/ppermute | solution.py:28
  48.1 41.7 %psum.70 = f32[4,512]{1,0:T(4,128)S(1)} all-reduce(f32[4,512]{1,0:T(4,128)S(1)} %reshape.145), channel_id=1, replica_groups=mesh['layer'=4,'row'=4,'col'=2] {'layer','row','col'}, use_global_device_ids=true, to_apply=%region_2.3 | all-reduce | flops 2048 | bytes 16384 | tf_op jit(solution)/shard_map/psum | solution.py:117
  92.6 4.2 %all-gather = f32[2,1,256]{2,1,0:T(1,128)S(1)} all-gather(f32[1,1,256]{2,1,0:T(1,128)S(1)} %bitcast.242), channel_id=1, replica_groups=mesh['layer'=4,'row'=4,'col'=2] {'col'}, dimensions={0}, use_global_device_ids=true | all-gather | bytes 3072 | tf_op jit(solution)/shard_map/all_gather | solution.py:124
  97.4 4.2 %all-gather.1 = f32[2,1,256]{2,1,0:T(1,128)S(1)} all-gather(f32[1,1,256]{2,1,0:T(1,128)S(1)} %bitcast.243), channel_id=1, replica_groups=mesh['layer'=4,'row'=4,'col'=2] {'col'}, dimensions={0}, use_global_device_ids=true | all-gather | bytes 3072 | tf_op jit(solution)/shard_map/all_gather | solution.py:124
  102.7 4.2 %all-gather.2 = f32[2,1,256]{2,1,0:T(1,128)S(1)} all-gather(f32[1,1,256]{2,1,0:T(1,128)S(1)} %bitcast.244), channel_id=1, replica_groups=mesh['layer'=4,'row'=4,'col'=2] {'col'}, dimensions={0}, use_global_device_ids=true | all-gather | bytes 3072 | tf_op jit(solution)/shard_map/all_gather | solution.py:124
  107.7 4.9 %psum.71 = f32[512]{0:T(512)S(1)} all-reduce(f32[512]{0:T(512)S(1)} %dynamic_update_slice.27), channel_id=1, replica_groups=mesh['layer'=4,'row'=4,'col'=2] {'col'}, use_global_device_ids=true, to_apply=%region_3.4 | all-reduce | flops 512 | bytes 4096 | tf_op jit(solution)/shard_map/psum | solution.py:138
  113.3 4.9 %psum.72 = f32[512]{0:T(512)S(1)} all-reduce(f32[512]{0:T(512)S(1)} %sub.193), channel_id=1, replica_groups=mesh['layer'=4,'row'=4,'col'=2] {'col'}, use_global_device_ids=true, to_apply=%region_4.5 | all-reduce | flops 512 | bytes 4096 | tf_op jit(solution)/shard_map/psum | solution.py:138
  121.9 3.6 %collective-permute-start.13 = (f32[1,1,64,512]{3,2,1,0:T(8,128)S(1)}, f32[1,1,64,512]{3,2,1,0:T(8,128)S(1)}, u32[]{:S(2)}, u32[]{:S(2)}) collective-permute-start(f32[1,1,64,512]{3,2,1,0:T(8,128)S(1)} %get-tuple-element.53), channel_id=1, source_target_pairs={{8,0},{16,8},{24,16},{9,1},{17,9},{25,17},{10,2},{18,10},{26,18},{... | collective-permute-start | bytes 393224 | tf_op jit(solution)/shard_map/ppermute | solution.py:28
  142.2 6.3 %psum.73 = f32[512]{0:T(512)S(1)} all-reduce(f32[512]{0:T(512)S(1)} %sub.194), channel_id=1, replica_groups=mesh['layer'=4,'row'=4,'col'=2] {'col'}, use_global_device_ids=true, to_apply=%region_5.6 | all-reduce | flops 512 | bytes 4096 | tf_op jit(solution)/shard_map/psum | solution.py:138
  157.8 3.6 %collective-permute-start.19 = (f32[1,1,64,512]{3,2,1,0:T(8,128)}, f32[1,1,64,512]{3,2,1,0:T(8,128)}, u32[]{:S(2)}, u32[]{:S(2)}) collective-permute-start(f32[1,1,64,512]{3,2,1,0:T(8,128)} %get-tuple-element.51), channel_id=1, source_target_pairs={{8,0},{16,8},{24,16},{9,1},{17,9},{25,17},{10,2},{18,10},{26,18},{... | collective-permute-start | bytes 393224 | tf_op jit(solution)/shard_map/ppermute | solution.py:28
  161.9 4.9 %psum.74 = f32[1,512]{1,0:T(1,128)S(1)} all-reduce(f32[1,512]{1,0:T(1,128)S(1)} %bitcast.217), channel_id=1, replica_groups=mesh['layer'=4,'row'=4,'col'=2] {'col'}, use_global_device_ids=true, to_apply=%region_6.7 | all-reduce | flops 512 | bytes 4096 | tf_op jit(solution)/shard_map/psum | solution.py:138
  172.4 4.2 %collective-permute-done.21 = f32[1,4,1,512]{3,2,1,0:T(1,128)S(1)} collective-permute-done((f32[1,4,1,512]{3,2,1,0:T(1,128)S(1)}, f32[1,4,1,512]{3,2,1,0:T(1,128)S(1)}, u32[]{:S(2)}, u32[]{:S(2)}) %collective-permute-start.21) | collective-permute-done | bytes 8224 | tf_op jit(solution)/shard_map/ppermute | solution.py:28
  177.6 4.0 %collective-permute-start.22 = (f32[1,4,66,1]{3,2,1,0:T(8,128)S(1)}, f32[1,4,66,1]{3,2,1,0:T(8,128)S(1)}, u32[]{:S(2)}, u32[]{:S(2)}) collective-permute-start(f32[1,4,66,1]{3,2,1,0:T(8,128)S(1)} %get-tuple-element.24), channel_id=1, source_target_pairs={{0,1},{2,3},{4,5},{6,7},{8,9},{10,11},{12,13},{14,15},{16,17},{18,... | collective-permute-start | bytes 3176 | tf_op jit(solution)/shard_map/ppermute | solution.py:26
  202.9 4.2 %collective-permute-done.27 = f32[1,4,1,512]{3,2,1,0:T(1,128)S(1)} collective-permute-done((f32[1,4,1,512]{3,2,1,0:T(1,128)S(1)}, f32[1,4,1,512]{3,2,1,0:T(1,128)S(1)}, u32[]{:S(2)}, u32[]{:S(2)}) %collective-permute-start.27) | collective-permute-done | bytes 8224 | tf_op jit(solution)/shard_map/ppermute | solution.py:28
  211.3 4.4 %collective-permute-done.29 = f32[1,4,66,1]{3,2,1,0:T(8,128)S(1)} collective-permute-done((f32[1,4,66,1]{3,2,1,0:T(8,128)S(1)}, f32[1,4,66,1]{3,2,1,0:T(8,128)S(1)}, u32[]{:S(2)}, u32[]{:S(2)}) %collective-permute-start.29) | collective-permute-done | bytes 1088 | tf_op jit(solution)/shard_map/ppermute | solution.py:28
  219.8 38.1 %psum.75 = f32[4,512]{1,0:T(4,128)S(1)} all-reduce(f32[4,512]{1,0:T(4,128)S(1)} %reshape.146), channel_id=1, replica_groups=mesh['layer'=4,'row'=4,'col'=2] {'layer','row','col'}, use_global_device_ids=true, to_apply=%region_9.10 | all-reduce | flops 2048 | bytes 16384 | tf_op jit(solution)/shard_map/psum | solution.py:117
  260.8 4.2 %all-gather.3 = f32[2,1,256]{2,1,0:T(1,128)S(1)} all-gather(f32[1,1,256]{2,1,0:T(1,128)S(1)} %bitcast.245), channel_id=1, replica_groups=mesh['layer'=4,'row'=4,'col'=2] {'col'}, dimensions={0}, use_global_device_ids=true | all-gather | bytes 3072 | tf_op jit(solution)/shard_map/all_gather | solution.py:124
  265.5 4.2 %all-gather.4 = f32[2,1,256]{2,1,0:T(1,128)S(1)} all-gather(f32[1,1,256]{2,1,0:T(1,128)S(1)} %bitcast.246), channel_id=1, replica_groups=mesh['layer'=4,'row'=4,'col'=2] {'col'}, dimensions={0}, use_global_device_ids=true | all-gather | bytes 3072 | tf_op jit(solution)/shard_map/all_gather | solution.py:124
  270.8 4.2 %all-gather.5 = f32[2,1,256]{2,1,0:T(1,128)S(1)} all-gather(f32[1,1,256]{2,1,0:T(1,128)S(1)} %bitcast.247), channel_id=1, replica_groups=mesh['layer'=4,'row'=4,'col'=2] {'col'}, dimensions={0}, use_global_device_ids=true | all-gather | bytes 3072 | tf_op jit(solution)/shard_map/all_gather | solution.py:124
  275.8 4.9 %psum.76 = f32[512]{0:T(512)S(1)} all-reduce(f32[512]{0:T(512)S(1)} %dynamic_update_slice.31), channel_id=1, replica_groups=mesh['layer'=4,'row'=4,'col'=2] {'col'}, use_global_device_ids=true, to_apply=%region_10.11 | all-reduce | flops 512 | bytes 4096 | tf_op jit(solution)/shard_map/psum | solution.py:138
  281.4 5.1 %psum.77 = f32[512]{0:T(512)S(1)} all-reduce(f32[512]{0:T(512)S(1)} %sub.220), channel_id=1, replica_groups=mesh['layer'=4,'row'=4,'col'=2] {'col'}, use_global_device_ids=true, to_apply=%region_11.12 | all-reduce | flops 512 | bytes 4096 | tf_op jit(solution)/shard_map/psum | solution.py:138
  290.2 3.6 %collective-permute-start.31 = (f32[1,1,64,512]{3,2,1,0:T(8,128)S(1)}, f32[1,1,64,512]{3,2,1,0:T(8,128)S(1)}, u32[]{:S(2)}, u32[]{:S(2)}) collective-permute-start(f32[1,1,64,512]{3,2,1,0:T(8,128)S(1)} %get-tuple-element.47), channel_id=1, source_target_pairs={{8,0},{16,8},{24,16},{9,1},{17,9},{25,17},{10,2},{18,10},{26,18},{... | collective-permute-start | bytes 393224 | tf_op jit(solution)/shard_map/ppermute | solution.py:28
  296.4 3.8 %collective-permute-start.32 = (f32[1,4,1,512]{3,2,1,0:T(1,128)S(1)}, f32[1,4,1,512]{3,2,1,0:T(1,128)S(1)}, u32[]{:S(2)}, u32[]{:S(2)}) collective-permute-start(f32[1,4,1,512]{3,2,1,0:T(1,128)S(1)} %get-tuple-element.32), channel_id=1, source_target_pairs={{0,2},{2,4},{4,6},{1,3},{3,5},{5,7},{8,10},{10,12},{12,14},{9,11},... | collective-permute-start | bytes 24584 | tf_op jit(solution)/shard_map/ppermute | solution.py:26
  306.5 3.9 %collective-permute-start.34 = (f32[1,4,66,1]{3,2,1,0:T(8,128)}, f32[1,4,66,1]{3,2,1,0:T(8,128)S(1)}, u32[]{:S(2)}, u32[]{:S(2)}) collective-permute-start(f32[1,4,66,1]{3,2,1,0:T(8,128)} %get-tuple-element.20), channel_id=1, source_target_pairs={{0,1},{2,3},{4,5},{6,7},{8,9},{10,11},{12,13},{14,15},{16,17},{18,... | collective-permute-start | bytes 3176 | tf_op jit(solution)/shard_map/ppermute | solution.py:26
  311.7 6.2 %psum.78 = f32[512]{0:T(512)S(1)} all-reduce(f32[512]{0:T(512)S(1)} %sub.221), channel_id=1, replica_groups=mesh['layer'=4,'row'=4,'col'=2] {'col'}, use_global_device_ids=true, to_apply=%region_12.13 | all-reduce | flops 512 | bytes 4096 | tf_op jit(solution)/shard_map/psum | solution.py:138
  325.0 3.6 %collective-permute-start.37 = (f32[1,1,64,512]{3,2,1,0:T(8,128)}, f32[1,1,64,512]{3,2,1,0:T(8,128)}, u32[]{:S(2)}, u32[]{:S(2)}) collective-permute-start(f32[1,1,64,512]{3,2,1,0:T(8,128)} %get-tuple-element.45), channel_id=1, source_target_pairs={{8,0},{16,8},{24,16},{9,1},{17,9},{25,17},{10,2},{18,10},{26,18},{... | collective-permute-start | bytes 393224 | tf_op jit(solution)/shard_map/ppermute | solution.py:28
  329.3 4.9 %psum.79 = f32[1,512]{1,0:T(1,128)S(1)} all-reduce(f32[1,512]{1,0:T(1,128)S(1)} %bitcast.218), channel_id=1, replica_groups=mesh['layer'=4,'row'=4,'col'=2] {'col'}, use_global_device_ids=true, to_apply=%region_13.14 | all-reduce | flops 512 | bytes 4096 | tf_op jit(solution)/shard_map/psum | solution.py:138
  344.2 4.0 %collective-permute-start.40 = (f32[1,4,66,1]{3,2,1,0:T(8,128)S(1)}, f32[1,4,66,1]{3,2,1,0:T(8,128)S(1)}, u32[]{:S(2)}, u32[]{:S(2)}) collective-permute-start(f32[1,4,66,1]{3,2,1,0:T(8,128)S(1)} %get-tuple-element.18), channel_id=1, source_target_pairs={{0,1},{2,3},{4,5},{6,7},{8,9},{10,11},{12,13},{14,15},{16,17},{18,... | collective-permute-start | bytes 3176 | tf_op jit(solution)/shard_map/ppermute | solution.py:26
  350.8 4.4 %collective-permute-done.41 = f32[1,4,66,1]{3,2,1,0:T(8,128)S(1)} collective-permute-done((f32[1,4,66,1]{3,2,1,0:T(8,128)S(1)}, f32[1,4,66,1]{3,2,1,0:T(8,128)S(1)}, u32[]{:S(2)}, u32[]{:S(2)}) %collective-permute-start.41) | collective-permute-done | bytes 1088 | tf_op jit(solution)/shard_map/ppermute | solution.py:28
  (313 shorter events, 144.0 us)
Async XLA Ops:
  0.7 12.3 %collective-permute-start.7 = (f32[1,1,64,512]{3,2,1,0:T(8,128)S(1)}, f32[1,1,64,512]{3,2,1,0:T(8,128)S(1)}, u32[]{:S(2)}, u32[]{:S(2)}) collective-permute-start(f32[1,1,64,512]{3,2,1,0:T(8,128)S(1)} %broadcast.185), channel_id=1, source_target_pairs={{8,0},{16,8},{24,16},{9,1},{17,9},{25,17},{10,2},{18,10},{26,18},{... | collective-permute-start | bytes 393224 | tf_op jit(solution)/shard_map/ppermute | solution.py:28
  2.7 10.3 %collective-permute-start.6 = (f32[1,1,64,512]{3,2,1,0:T(8,128)S(1)}, f32[1,1,64,512]{3,2,1,0:T(8,128)S(1)}, u32[]{:S(2)}, u32[]{:S(2)}) collective-permute-start(f32[1,1,64,512]{3,2,1,0:T(8,128)S(1)} %broadcast.185), channel_id=1, source_target_pairs={{0,8},{8,16},{16,24},{1,9},{9,17},{17,25},{2,10},{10,18},{18,26},{... | collective-permute-start | bytes 393224 | tf_op jit(solution)/shard_map/ppermute | solution.py:26
  7.2 10.6 %collective-permute-start = (f32[2,1,64,512]{3,2,1,0:T(8,128)S(1)}, f32[2,1,64,512]{3,2,1,0:T(8,128)S(1)}, u32[]{:S(2)}, u32[]{:S(2)}) collective-permute-start(f32[2,1,64,512]{3,2,1,0:T(8,128)S(1)} %get-tuple-element.40), channel_id=1, source_target_pairs={{0,8},{8,16},{16,24},{1,9},{9,17},{17,25},{2,10},{10,18},{18,26},{... | collective-permute-start | bytes 786440 | tf_op jit(solution)/shard_map/ppermute | solution.py:26
  9.2 8.7 %collective-permute-start.1 = (f32[2,1,64,512]{3,2,1,0:T(8,128)S(1)}, f32[2,1,64,512]{3,2,1,0:T(8,128)S(1)}, u32[]{:S(2)}, u32[]{:S(2)}) collective-permute-start(f32[2,1,64,512]{3,2,1,0:T(8,128)S(1)} %get-tuple-element.41), channel_id=1, source_target_pairs={{8,0},{16,8},{24,16},{9,1},{17,9},{25,17},{10,2},{18,10},{26,18},{... | collective-permute-start | bytes 786440 | tf_op jit(solution)/shard_map/ppermute | solution.py:28
  13.1 10.7 %collective-permute-start.8 = (f32[1,4,1,512]{3,2,1,0:T(1,128)S(1)}, f32[1,4,1,512]{3,2,1,0:T(1,128)S(1)}, u32[]{:S(2)}, u32[]{:S(2)}) collective-permute-start(f32[1,4,1,512]{3,2,1,0:T(1,128)S(1)} %get-tuple-element.42), channel_id=1, source_target_pairs={{0,2},{2,4},{4,6},{1,3},{3,5},{5,7},{8,10},{10,12},{12,14},{9,11},... | collective-permute-start | bytes 24584 | tf_op jit(solution)/shard_map/ppermute | solution.py:26
  16.5 7.2 %collective-permute-start.9 = (f32[1,4,1,512]{3,2,1,0:T(1,128)S(1)}, f32[1,4,1,512]{3,2,1,0:T(1,128)S(1)}, u32[]{:S(2)}, u32[]{:S(2)}) collective-permute-start(f32[1,4,1,512]{3,2,1,0:T(1,128)S(1)} %get-tuple-element.43), channel_id=1, source_target_pairs={{2,0},{4,2},{6,4},{3,1},{5,3},{7,5},{10,8},{12,10},{14,12},{11,9},... | collective-permute-start | bytes 24584 | tf_op jit(solution)/shard_map/ppermute | solution.py:28
  17.9 10.7 %collective-permute-start.2 = (f32[2,4,1,512]{3,2,1,0:T(1,128)S(1)}, f32[2,4,1,512]{3,2,1,0:T(1,128)S(1)}, u32[]{:S(2)}, u32[]{:S(2)}) collective-permute-start(f32[2,4,1,512]{3,2,1,0:T(1,128)S(1)} %get-tuple-element.16), channel_id=1, source_target_pairs={{0,2},{2,4},{4,6},{1,3},{3,5},{5,7},{8,10},{10,12},{12,14},{9,11},... | collective-permute-start | bytes 49160 | tf_op jit(solution)/shard_map/ppermute | solution.py:26
  22.5 6.2 %collective-permute-start.3 = (f32[2,4,1,512]{3,2,1,0:T(1,128)S(1)}, f32[2,4,1,512]{3,2,1,0:T(1,128)S(1)}, u32[]{:S(2)}, u32[]{:S(2)}) collective-permute-start(f32[2,4,1,512]{3,2,1,0:T(1,128)S(1)} %get-tuple-element.17), channel_id=1, source_target_pairs={{2,0},{4,2},{6,4},{3,1},{5,3},{7,5},{10,8},{12,10},{14,12},{11,9},... | collective-permute-start | bytes 49160 | tf_op jit(solution)/shard_map/ppermute | solution.py:28
  23.9 10.8 %collective-permute-start.10 = (f32[1,4,66,1]{3,2,1,0:T(8,128)S(1)}, f32[1,4,66,1]{3,2,1,0:T(8,128)S(1)}, u32[]{:S(2)}, u32[]{:S(2)}) collective-permute-start(f32[1,4,66,1]{3,2,1,0:T(8,128)S(1)} %get-tuple-element.28), channel_id=1, source_target_pairs={{0,1},{2,3},{4,5},{6,7},{8,9},{10,11},{12,13},{14,15},{16,17},{18,... | collective-permute-start | bytes 3176 | tf_op jit(solution)/shard_map/ppermute | solution.py:26
  27.4 7.4 %collective-permute-start.11 = (f32[1,4,66,1]{3,2,1,0:T(8,128)S(1)}, f32[1,4,66,1]{3,2,1,0:T(8,128)S(1)}, u32[]{:S(2)}, u32[]{:S(2)}) collective-permute-start(f32[1,4,66,1]{3,2,1,0:T(8,128)S(1)} %get-tuple-element.29), channel_id=1, source_target_pairs={{1,0},{3,2},{5,4},{7,6},{9,8},{11,10},{13,12},{15,14},{17,16},{19,... | collective-permute-start | bytes 3176 | tf_op jit(solution)/shard_map/ppermute | solution.py:28
  28.8 8.8 %collective-permute-start.4 = (f32[2,4,66,1]{3,2,1,0:T(8,128)S(1)}, f32[2,4,66,1]{3,2,1,0:T(8,128)S(1)}, u32[]{:S(2)}, u32[]{:S(2)}) collective-permute-start(f32[2,4,66,1]{3,2,1,0:T(8,128)S(1)} %get-tuple-element.14), channel_id=1, source_target_pairs={{0,1},{2,3},{4,5},{6,7},{8,9},{10,11},{12,13},{14,15},{16,17},{18,... | collective-permute-start | bytes 6344 | tf_op jit(solution)/shard_map/ppermute | solution.py:26
  33.4 8.6 %collective-permute-start.5 = (f32[2,4,66,1]{3,2,1,0:T(8,128)S(1)}, f32[2,4,66,1]{3,2,1,0:T(8,128)S(1)}, u32[]{:S(2)}, u32[]{:S(2)}) collective-permute-start(f32[2,4,66,1]{3,2,1,0:T(8,128)S(1)} %get-tuple-element.15), channel_id=1, source_target_pairs={{1,0},{3,2},{5,4},{7,6},{9,8},{11,10},{13,12},{15,14},{17,16},{19,... | collective-permute-start | bytes 6344 | tf_op jit(solution)/shard_map/ppermute | solution.py:28
  119.9 7.7 %collective-permute-start.12 = (f32[1,1,64,512]{3,2,1,0:T(8,128)S(1)}, f32[1,1,64,512]{3,2,1,0:T(8,128)S(1)}, u32[]{:S(2)}, u32[]{:S(2)}) collective-permute-start(f32[1,1,64,512]{3,2,1,0:T(8,128)S(1)} %get-tuple-element.52), channel_id=1, source_target_pairs={{0,8},{8,16},{16,24},{1,9},{9,17},{17,25},{2,10},{10,18},{18,26},{... | collective-permute-start | bytes 393224 | tf_op jit(solution)/shard_map/ppermute | solution.py:26
  121.9 6.1 %collective-permute-start.13 = (f32[1,1,64,512]{3,2,1,0:T(8,128)S(1)}, f32[1,1,64,512]{3,2,1,0:T(8,128)S(1)}, u32[]{:S(2)}, u32[]{:S(2)}) collective-permute-start(f32[1,1,64,512]{3,2,1,0:T(8,128)S(1)} %get-tuple-element.53), channel_id=1, source_target_pairs={{8,0},{16,8},{24,16},{9,1},{17,9},{25,17},{10,2},{18,10},{26,18},{... | collective-permute-start | bytes 393224 | tf_op jit(solution)/shard_map/ppermute | solution.py:28
  137.8 12.2 %collective-permute-start.16 = (f32[1,4,66,1]{3,2,1,0:T(8,128)}, f32[1,4,66,1]{3,2,1,0:T(8,128)S(1)}, u32[]{:S(2)}, u32[]{:S(2)}) collective-permute-start(f32[1,4,66,1]{3,2,1,0:T(8,128)} %get-tuple-element.26), channel_id=1, source_target_pairs={{0,1},{2,3},{4,5},{6,7},{8,9},{10,11},{12,13},{14,15},{16,17},{18,... | collective-permute-start | bytes 3176 | tf_op jit(solution)/shard_map/ppermute | solution.py:26
  140.9 10.3 %collective-permute-start.17 = (f32[1,4,66,1]{3,2,1,0:T(8,128)}, f32[1,4,66,1]{3,2,1,0:T(8,128)}, u32[]{:S(2)}, u32[]{:S(2)}) collective-permute-start(f32[1,4,66,1]{3,2,1,0:T(8,128)} %get-tuple-element.27), channel_id=1, source_target_pairs={{1,0},{3,2},{5,4},{7,6},{9,8},{11,10},{13,12},{15,14},{17,16},{19,... | collective-permute-start | bytes 3176 | tf_op jit(solution)/shard_map/ppermute | solution.py:28
  155.9 10.9 %collective-permute-start.18 = (f32[1,1,64,512]{3,2,1,0:T(8,128)}, f32[1,1,64,512]{3,2,1,0:T(8,128)}, u32[]{:S(2)}, u32[]{:S(2)}) collective-permute-start(f32[1,1,64,512]{3,2,1,0:T(8,128)} %get-tuple-element.50), channel_id=1, source_target_pairs={{0,8},{8,16},{16,24},{1,9},{9,17},{17,25},{2,10},{10,18},{18,26},{... | collective-permute-start | bytes 393224 | tf_op jit(solution)/shard_map/ppermute | solution.py:26
  157.8 9.0 %collective-permute-start.19 = (f32[1,1,64,512]{3,2,1,0:T(8,128)}, f32[1,1,64,512]{3,2,1,0:T(8,128)}, u32[]{:S(2)}, u32[]{:S(2)}) collective-permute-start(f32[1,1,64,512]{3,2,1,0:T(8,128)} %get-tuple-element.51), channel_id=1, source_target_pairs={{8,0},{16,8},{24,16},{9,1},{17,9},{25,17},{10,2},{18,10},{26,18},{... | collective-permute-start | bytes 393224 | tf_op jit(solution)/shard_map/ppermute | solution.py:28
  177.6 7.5 %collective-permute-start.22 = (f32[1,4,66,1]{3,2,1,0:T(8,128)S(1)}, f32[1,4,66,1]{3,2,1,0:T(8,128)S(1)}, u32[]{:S(2)}, u32[]{:S(2)}) collective-permute-start(f32[1,4,66,1]{3,2,1,0:T(8,128)S(1)} %get-tuple-element.24), channel_id=1, source_target_pairs={{0,1},{2,3},{4,5},{6,7},{8,9},{10,11},{12,13},{14,15},{16,17},{18,... | collective-permute-start | bytes 3176 | tf_op jit(solution)/shard_map/ppermute | solution.py:26
  181.5 7.0 %collective-permute-start.23 = (f32[1,4,66,1]{3,2,1,0:T(8,128)S(1)}, f32[1,4,66,1]{3,2,1,0:T(8,128)S(1)}, u32[]{:S(2)}, u32[]{:S(2)}) collective-permute-start(f32[1,4,66,1]{3,2,1,0:T(8,128)S(1)} %get-tuple-element.25), channel_id=1, source_target_pairs={{1,0},{3,2},{5,4},{7,6},{9,8},{11,10},{13,12},{15,14},{17,16},{19,... | collective-permute-start | bytes 3176 | tf_op jit(solution)/shard_map/ppermute | solution.py:28
  191.0 6.4 %collective-permute-start.24 = (f32[1,1,64,512]{3,2,1,0:T(8,128)S(1)}, f32[1,1,64,512]{3,2,1,0:T(8,128)S(1)}, u32[]{:S(2)}, u32[]{:S(2)}) collective-permute-start(f32[1,1,64,512]{3,2,1,0:T(8,128)S(1)} %get-tuple-element.48), channel_id=1, source_target_pairs={{0,8},{8,16},{16,24},{1,9},{9,17},{17,25},{2,10},{10,18},{18,26},{... | collective-permute-start | bytes 393224 | tf_op jit(solution)/shard_map/ppermute | solution.py:26
  193.0 6.1 %collective-permute-start.25 = (f32[1,1,64,512]{3,2,1,0:T(8,128)S(1)}, f32[1,1,64,512]{3,2,1,0:T(8,128)S(1)}, u32[]{:S(2)}, u32[]{:S(2)}) collective-permute-start(f32[1,1,64,512]{3,2,1,0:T(8,128)S(1)} %get-tuple-element.49), channel_id=1, source_target_pairs={{8,0},{16,8},{24,16},{9,1},{17,9},{25,17},{10,2},{18,10},{26,18},{... | collective-permute-start | bytes 393224 | tf_op jit(solution)/shard_map/ppermute | solution.py:28
  208.7 7.0 %collective-permute-start.29 = (f32[1,4,66,1]{3,2,1,0:T(8,128)S(1)}, f32[1,4,66,1]{3,2,1,0:T(8,128)S(1)}, u32[]{:S(2)}, u32[]{:S(2)}) collective-permute-start(f32[1,4,66,1]{3,2,1,0:T(8,128)S(1)} %get-tuple-element.23), channel_id=1, source_target_pairs={{1,0},{3,2},{5,4},{7,6},{9,8},{11,10},{13,12},{15,14},{17,16},{19,... | collective-permute-start | bytes 3176 | tf_op jit(solution)/shard_map/ppermute | solution.py:28
  288.3 7.7 %collective-permute-start.30 = (f32[1,1,64,512]{3,2,1,0:T(8,128)S(1)}, f32[1,1,64,512]{3,2,1,0:T(8,128)S(1)}, u32[]{:S(2)}, u32[]{:S(2)}) collective-permute-start(f32[1,1,64,512]{3,2,1,0:T(8,128)S(1)} %get-tuple-element.46), channel_id=1, source_target_pairs={{0,8},{8,16},{16,24},{1,9},{9,17},{17,25},{2,10},{10,18},{18,26},{... | collective-permute-start | bytes 393224 | tf_op jit(solution)/shard_map/ppermute | solution.py:26
  290.2 6.1 %collective-permute-start.31 = (f32[1,1,64,512]{3,2,1,0:T(8,128)S(1)}, f32[1,1,64,512]{3,2,1,0:T(8,128)S(1)}, u32[]{:S(2)}, u32[]{:S(2)}) collective-permute-start(f32[1,1,64,512]{3,2,1,0:T(8,128)S(1)} %get-tuple-element.47), channel_id=1, source_target_pairs={{8,0},{16,8},{24,16},{9,1},{17,9},{25,17},{10,2},{18,10},{26,18},{... | collective-permute-start | bytes 393224 | tf_op jit(solution)/shard_map/ppermute | solution.py:28
  296.4 6.3 %collective-permute-start.32 = (f32[1,4,1,512]{3,2,1,0:T(1,128)S(1)}, f32[1,4,1,512]{3,2,1,0:T(1,128)S(1)}, u32[]{:S(2)}, u32[]{:S(2)}) collective-permute-start(f32[1,4,1,512]{3,2,1,0:T(1,128)S(1)} %get-tuple-element.32), channel_id=1, source_target_pairs={{0,2},{2,4},{4,6},{1,3},{3,5},{5,7},{8,10},{10,12},{12,14},{9,11},... | collective-permute-start | bytes 24584 | tf_op jit(solution)/shard_map/ppermute | solution.py:26
  306.5 11.5 %collective-permute-start.34 = (f32[1,4,66,1]{3,2,1,0:T(8,128)}, f32[1,4,66,1]{3,2,1,0:T(8,128)S(1)}, u32[]{:S(2)}, u32[]{:S(2)}) collective-permute-start(f32[1,4,66,1]{3,2,1,0:T(8,128)} %get-tuple-element.20), channel_id=1, source_target_pairs={{0,1},{2,3},{4,5},{6,7},{8,9},{10,11},{12,13},{14,15},{16,17},{18,... | collective-permute-start | bytes 3176 | tf_op jit(solution)/shard_map/ppermute | solution.py:26
  310.4 8.7 %collective-permute-start.35 = (f32[1,4,66,1]{3,2,1,0:T(8,128)}, f32[1,4,66,1]{3,2,1,0:T(8,128)}, u32[]{:S(2)}, u32[]{:S(2)}) collective-permute-start(f32[1,4,66,1]{3,2,1,0:T(8,128)} %get-tuple-element.21), channel_id=1, source_target_pairs={{1,0},{3,2},{5,4},{7,6},{9,8},{11,10},{13,12},{15,14},{17,16},{19,... | collective-permute-start | bytes 3176 | tf_op jit(solution)/shard_map/ppermute | solution.py:28
  323.1 11.2 %collective-permute-start.36 = (f32[1,1,64,512]{3,2,1,0:T(8,128)}, f32[1,1,64,512]{3,2,1,0:T(8,128)}, u32[]{:S(2)}, u32[]{:S(2)}) collective-permute-start(f32[1,1,64,512]{3,2,1,0:T(8,128)} %get-tuple-element.44), channel_id=1, source_target_pairs={{0,8},{8,16},{16,24},{1,9},{9,17},{17,25},{2,10},{10,18},{18,26},{... | collective-permute-start | bytes 393224 | tf_op jit(solution)/shard_map/ppermute | solution.py:26
  325.0 9.3 %collective-permute-start.37 = (f32[1,1,64,512]{3,2,1,0:T(8,128)}, f32[1,1,64,512]{3,2,1,0:T(8,128)}, u32[]{:S(2)}, u32[]{:S(2)}) collective-permute-start(f32[1,1,64,512]{3,2,1,0:T(8,128)} %get-tuple-element.45), channel_id=1, source_target_pairs={{8,0},{16,8},{24,16},{9,1},{17,9},{25,17},{10,2},{18,10},{26,18},{... | collective-permute-start | bytes 393224 | tf_op jit(solution)/shard_map/ppermute | solution.py:28
  344.2 6.6 %collective-permute-start.40 = (f32[1,4,66,1]{3,2,1,0:T(8,128)S(1)}, f32[1,4,66,1]{3,2,1,0:T(8,128)S(1)}, u32[]{:S(2)}, u32[]{:S(2)}) collective-permute-start(f32[1,4,66,1]{3,2,1,0:T(8,128)S(1)} %get-tuple-element.18), channel_id=1, source_target_pairs={{0,1},{2,3},{4,5},{6,7},{8,9},{10,11},{12,13},{14,15},{16,17},{18,... | collective-permute-start | bytes 3176 | tf_op jit(solution)/shard_map/ppermute | solution.py:26
  348.2 7.0 %collective-permute-start.41 = (f32[1,4,66,1]{3,2,1,0:T(8,128)S(1)}, f32[1,4,66,1]{3,2,1,0:T(8,128)S(1)}, u32[]{:S(2)}, u32[]{:S(2)}) collective-permute-start(f32[1,4,66,1]{3,2,1,0:T(8,128)S(1)} %get-tuple-element.19), channel_id=1, source_target_pairs={{1,0},{3,2},{5,4},{7,6},{9,8},{11,10},{13,12},{15,14},{17,16},{19,... | collective-permute-start | bytes 3176 | tf_op jit(solution)/shard_map/ppermute | solution.py:28
  (73 other events, 1157.3 us)
where the time goes:
time: 360 us; the launch traced here: 358 us
  blocking collectives  148 us (41%)
  starting transfers between devices  104 us (29%)
  waiting for transfers between devices  41.1 us (11%)
  other arithmetic  26.6 us (7%)
  matrix products  25.4 us (7%)
  local copies, waits for them, and re-layouts  11.5 us (3%)
    psum x2, blocking collectives, shards(): rhs = lax.psum(local_rhs, ('layer', 'row', 'col')) * (restrict_scale / TILE)  79.9 us
    ppermute x21, starting transfers between devices, padded(): lax.ppermute(tail, axis, [(i, (i + 1) % count) for i in range(ends)])  61.9 us
    psum x8, blocking collectives, shards(): results[section] = lax.psum(placed, 'col')  42.2 us
    ppermute x21, starting transfers between devices, padded(): lax.ppermute(head, axis, [((i + 1) % count, i) for i in range(ends)])  42 us
    ppermute x21, waiting for transfers between devices, padded(): lax.ppermute(head, axis, [((i + 1) % count, i) for i in range(ends)])  35.7 us
    all_gather x6, blocking collectives, shards(): full = lax.all_gather(piece, 'col', axis=0, tiled=True)  25.4 us
    dot_general x8, matrix products, shards(): jnp.dot(pivots[section], forward[section], precision=highest)  10.7 us
  transfers between devices with their start and end apart: 42, of which 16 were waited for; matrix products, arithmetic and copies ran while one was open for 5% of the time, Pallas kernels for 0%

commit v1 on v0

--- a/solution.py
+++ b/solution.py
@@ -13,6 +13,10 @@
 bound_high = 1.9
 restrict_scale = 0.25
 prolong_scale = 0.5
+
+
+def assign_the_slices(base_x, bus_axis):
+    return jax.lax.all_gather(base_x, bus_axis).sum(axis=0)
 
 
 def padded(cells, sides, width):
@@ -114,7 +118,7 @@
         plane = jnp.sum(resid, axis=0)
         row_sums = jnp.dot(row_select, plane, precision=highest)
         local_rhs = jnp.sum(row_sums * col_select, axis=1).reshape(NPANEL, PANEL)
-        rhs = lax.psum(local_rhs, ("layer", "row", "col")) * (restrict_scale / TILE)
+        rhs = assign_the_slices(local_rhs, ("layer", "row", "col")) * (restrict_scale / TILE)
         full = rhs[0]
         forward = [full]
         for section in range(1, NPANEL):

time: 360 us -> 403 us (1.12)
  blocking collectives: 148 us -> 199 us
  starting transfers between devices: 104 us -> 95.5 us
    all_gather x0 -> x2, blocking collectives: none -> 131 us  [assign_the_slices(): return jax.lax.all_gather(base_x, bus_axis).sum(axis=0)]
    psum x2 -> x0, blocking collectives: 79.9 us -> none  [shards(): rhs = lax.psum(local_rhs, ('layer', 'row', 'col')) * (restrict_scale / TILE)]
    ppermute x21, starting transfers between devices: 61.9 us -> 53.3 us  [padded(): lax.ppermute(tail, axis, [(i, (i + 1) % count) for i in range(ends)])]
  transfers between devices with their start and end apart: 42 -> 42, of which waited for: 16 -> 16; matrix products, arithmetic and copies ran while one was open for 5% -> 4% of each run, Pallas kernels for 0% -> 0%
where the time goes in v1:
time: 403 us; the launch traced here: 402 us
  blocking collectives  199 us (49%)
  starting transfers between devices  95.5 us (24%)
  waiting for transfers between devices  41.1 us (10%)
  other arithmetic  26.7 us (7%)
  matrix products  25.4 us (6%)
  local copies, waits for them, and re-layouts  11.5 us (3%)
    all_gather x2, blocking collectives, assign_the_slices(): return jax.lax.all_gather(base_x, bus_axis).sum(axis=0)  131 us
    ppermute x21, starting transfers between devices, padded(): lax.ppermute(tail, axis, [(i, (i + 1) % count) for i in range(ends)])  53.3 us
    ppermute x21, starting transfers between devices, padded(): lax.ppermute(head, axis, [((i + 1) % count, i) for i in range(ends)])  42.2 us
    psum x8, blocking collectives, shards(): results[section] = lax.psum(placed, 'col')  42.1 us
    ppermute x21, waiting for transfers between devices, padded(): lax.ppermute(head, axis, [((i + 1) % count, i) for i in range(ends)])  35.7 us
    all_gather x6, blocking collectives, shards(): full = lax.all_gather(piece, 'col', axis=0, tiled=True)  25.7 us
    dot_general x8, matrix products, shards(): jnp.dot(pivots[section], forward[section], precision=highest)  10.7 us
  transfers between devices with their start and end apart: 42, of which 16 were waited for; matrix products, arithmetic and copies ran while one was open for 4% of the time, Pallas kernels for 0%

profile of v1, /device:TPU:2, one launch (start us, length us, event | category | flops | bytes accessed | tf_op | source)
XLA Modules:
  0.0 401.6 jit_solution(6283689891811974102)
XLA Ops:
  9.2 3.6 collective-permute-start.1
  17.9 4.5 %collective-permute-start.2 = (f32[2,4,1,512]{3,2,1,0:T(1,128)S(1)}, f32[2,4,1,512]{3,2,1,0:T(1,128)S(1)}, u32[]{:S(2)}, u32[]{:S(2)}) collective-permute-start(f32[2,4,1,512]{3,2,1,0:T(1,128)S(1)} %get-tuple-element.16), channel_id=1, source_target_pairs={{0,2},{2,4},{4,6},{1,3},{3,5},{5,7},{8,10},{10,12},{12,14},{9,11},... | collective-permute-start | bytes 49160 | tf_op jit(solution)/shard_map/ppermute | solution.py:30
  28.8 4.6 %collective-permute-start.4 = (f32[2,4,66,1]{3,2,1,0:T(8,128)S(1)}, f32[2,4,66,1]{3,2,1,0:T(8,128)S(1)}, u32[]{:S(2)}, u32[]{:S(2)}) collective-permute-start(f32[2,4,66,1]{3,2,1,0:T(8,128)S(1)} %get-tuple-element.14), channel_id=1, source_target_pairs={{0,1},{2,3},{4,5},{6,7},{8,9},{10,11},{12,13},{14,15},{16,17},{18,... | collective-permute-start | bytes 6344 | tf_op jit(solution)/shard_map/ppermute | solution.py:30
  37.6 4.4 %collective-permute-done.5 = f32[2,4,66,1]{3,2,1,0:T(8,128)S(1)} collective-permute-done((f32[2,4,66,1]{3,2,1,0:T(8,128)S(1)}, f32[2,4,66,1]{3,2,1,0:T(8,128)S(1)}, u32[]{:S(2)}, u32[]{:S(2)}) %collective-permute-start.5) | collective-permute-done | bytes 2144 | tf_op jit(solution)/shard_map/ppermute | solution.py:32
  48.1 66.8 %all_gather.24 = f32[32,4,512]{2,1,0:T(4,128)S(1)} all-gather(f32[1,4,512]{2,1,0:T(4,128)S(1)} %all_gather_reshape.6), channel_id=1, replica_groups=mesh['layer'=4,'row'=4,'col'=2] {'layer','row','col'}, dimensions={0}, use_global_device_ids=true | all-gather | bytes 270336 | tf_op jit(solution)/shard_map/all_gather | solution.py:19
  117.7 4.2 %all-gather = f32[2,1,256]{2,1,0:T(1,128)S(1)} all-gather(f32[1,1,256]{2,1,0:T(1,128)S(1)} %bitcast.242), channel_id=1, replica_groups=mesh['layer'=4,'row'=4,'col'=2] {'col'}, dimensions={0}, use_global_device_ids=true | all-gather | bytes 3072 | tf_op jit(solution)/shard_map/all_gather | solution.py:128
  122.5 4.2 %all-gather.1 = f32[2,1,256]{2,1,0:T(1,128)S(1)} all-gather(f32[1,1,256]{2,1,0:T(1,128)S(1)} %bitcast.243), channel_id=1, replica_groups=mesh['layer'=4,'row'=4,'col'=2] {'col'}, dimensions={0}, use_global_device_ids=true | all-gather | bytes 3072 | tf_op jit(solution)/shard_map/all_gather | solution.py:128
  127.8 4.2 %all-gather.2 = f32[2,1,256]{2,1,0:T(1,128)S(1)} all-gather(f32[1,1,256]{2,1,0:T(1,128)S(1)} %bitcast.244), channel_id=1, replica_groups=mesh['layer'=4,'row'=4,'col'=2] {'col'}, dimensions={0}, use_global_device_ids=true | all-gather | bytes 3072 | tf_op jit(solution)/shard_map/all_gather | solution.py:128
  132.8 4.9 %psum.56 = f32[512]{0:T(512)S(1)} all-reduce(f32[512]{0:T(512)S(1)} %dynamic_update_slice.27), channel_id=1, replica_groups=mesh['layer'=4,'row'=4,'col'=2] {'col'}, use_global_device_ids=true, to_apply=%region_3.4 | all-reduce | flops 512 | bytes 4096 | tf_op jit(solution)/shard_map/psum | solution.py:142
  138.3 4.9 %psum.57 = f32[512]{0:T(512)S(1)} all-reduce(f32[512]{0:T(512)S(1)} %sub.193), channel_id=1, replica_groups=mesh['layer'=4,'row'=4,'col'=2] {'col'}, use_global_device_ids=true, to_apply=%region_4.5 | all-reduce | flops 512 | bytes 4096 | tf_op jit(solution)/shard_map/psum | solution.py:142
  146.9 3.6 collective-permute-start.13
  164.2 6.2 %psum.58 = f32[512]{0:T(512)S(1)} all-reduce(f32[512]{0:T(512)S(1)} %sub.194), channel_id=1, replica_groups=mesh['layer'=4,'row'=4,'col'=2] {'col'}, use_global_device_ids=true, to_apply=%region_5.6 | all-reduce | flops 512 | bytes 4096 | tf_op jit(solution)/shard_map/psum | solution.py:142
  179.6 3.8 collective-permute-start.19
  183.8 4.9 %psum.59 = f32[1,512]{1,0:T(1,128)S(1)} all-reduce(f32[1,512]{1,0:T(1,128)S(1)} %bitcast.217), channel_id=1, replica_groups=mesh['layer'=4,'row'=4,'col'=2] {'col'}, use_global_device_ids=true, to_apply=%region_6.7 | all-reduce | flops 512 | bytes 4096 | tf_op jit(solution)/shard_map/psum | solution.py:142
  192.7 4.2 %collective-permute-done.21 = f32[1,4,1,512]{3,2,1,0:T(1,128)S(1)} collective-permute-done((f32[1,4,1,512]{3,2,1,0:T(1,128)S(1)}, f32[1,4,1,512]{3,2,1,0:T(1,128)S(1)}, u32[]{:S(2)}, u32[]{:S(2)}) %collective-permute-start.21) | collective-permute-done | bytes 8224 | tf_op jit(solution)/shard_map/ppermute | solution.py:32
  197.9 4.0 collective-permute-start.22
  213.3 3.6 collective-permute-start.25
  222.8 4.2 %collective-permute-done.27 = f32[1,4,1,512]{3,2,1,0:T(1,128)S(1)} collective-permute-done((f32[1,4,1,512]{3,2,1,0:T(1,128)S(1)}, f32[1,4,1,512]{3,2,1,0:T(1,128)S(1)}, u32[]{:S(2)}, u32[]{:S(2)}) %collective-permute-start.27) | collective-permute-done | bytes 8224 | tf_op jit(solution)/shard_map/ppermute | solution.py:32
  231.2 4.4 %collective-permute-done.29 = f32[1,4,66,1]{3,2,1,0:T(8,128)S(1)} collective-permute-done((f32[1,4,66,1]{3,2,1,0:T(8,128)S(1)}, f32[1,4,66,1]{3,2,1,0:T(8,128)S(1)}, u32[]{:S(2)}, u32[]{:S(2)}) %collective-permute-start.29) | collective-permute-done | bytes 1088 | tf_op jit(solution)/shard_map/ppermute | solution.py:32
  239.7 64.7 %all_gather.28 = f32[32,4,512]{2,1,0:T(4,128)S(1)} all-gather(f32[1,4,512]{2,1,0:T(4,128)S(1)} %all_gather_reshape.7), channel_id=1, replica_groups=mesh['layer'=4,'row'=4,'col'=2] {'layer','row','col'}, dimensions={0}, use_global_device_ids=true | all-gather | bytes 270336 | tf_op jit(solution)/shard_map/all_gather | solution.py:19
  307.3 4.5 %all-gather.3 = f32[2,1,256]{2,1,0:T(1,128)S(1)} all-gather(f32[1,1,256]{2,1,0:T(1,128)S(1)} %bitcast.245), channel_id=1, replica_groups=mesh['layer'=4,'row'=4,'col'=2] {'col'}, dimensions={0}, use_global_device_ids=true | all-gather | bytes 3072 | tf_op jit(solution)/shard_map/all_gather | solution.py:128
  312.3 4.2 %all-gather.4 = f32[2,1,256]{2,1,0:T(1,128)S(1)} all-gather(f32[1,1,256]{2,1,0:T(1,128)S(1)} %bitcast.246), channel_id=1, replica_groups=mesh['layer'=4,'row'=4,'col'=2] {'col'}, dimensions={0}, use_global_device_ids=true | all-gather | bytes 3072 | tf_op jit(solution)/shard_map/all_gather | solution.py:128
  317.6 4.2 %all-gather.5 = f32[2,1,256]{2,1,0:T(1,128)S(1)} all-gather(f32[1,1,256]{2,1,0:T(1,128)S(1)} %bitcast.247), channel_id=1, replica_groups=mesh['layer'=4,'row'=4,'col'=2] {'col'}, dimensions={0}, use_global_device_ids=true | all-gather | bytes 3072 | tf_op jit(solution)/shard_map/all_gather | solution.py:128
  322.6 4.9 %psum.60 = f32[512]{0:T(512)S(1)} all-reduce(f32[512]{0:T(512)S(1)} %dynamic_update_slice.31), channel_id=1, replica_groups=mesh['layer'=4,'row'=4,'col'=2] {'col'}, use_global_device_ids=true, to_apply=%region_10.11 | all-reduce | flops 512 | bytes 4096 | tf_op jit(solution)/shard_map/psum | solution.py:142
  328.2 4.9 %psum.61 = f32[512]{0:T(512)S(1)} all-reduce(f32[512]{0:T(512)S(1)} %sub.220), channel_id=1, replica_groups=mesh['layer'=4,'row'=4,'col'=2] {'col'}, use_global_device_ids=true, to_apply=%region_11.12 | all-reduce | flops 512 | bytes 4096 | tf_op jit(solution)/shard_map/psum | solution.py:142
  336.8 3.6 collective-permute-start.31
  350.6 3.9 collective-permute-start.34
  355.8 6.4 %psum.62 = f32[512]{0:T(512)S(1)} all-reduce(f32[512]{0:T(512)S(1)} %sub.221), channel_id=1, replica_groups=mesh['layer'=4,'row'=4,'col'=2] {'col'}, use_global_device_ids=true, to_apply=%region_12.13 | all-reduce | flops 512 | bytes 4096 | tf_op jit(solution)/shard_map/psum | solution.py:142
  369.3 3.6 collective-permute-start.37
  373.6 4.9 %psum.63 = f32[1,512]{1,0:T(1,128)S(1)} all-reduce(f32[1,512]{1,0:T(1,128)S(1)} %bitcast.218), channel_id=1, replica_groups=mesh['layer'=4,'row'=4,'col'=2] {'col'}, use_global_device_ids=true, to_apply=%region_13.14 | all-reduce | flops 512 | bytes 4096 | tf_op jit(solution)/shard_map/psum | solution.py:142
  387.6 4.0 collective-permute-start.40
  394.2 4.4 %collective-permute-done.41 = f32[1,4,66,1]{3,2,1,0:T(8,128)S(1)} collective-permute-done((f32[1,4,66,1]{3,2,1,0:T(8,128)S(1)}, f32[1,4,66,1]{3,2,1,0:T(8,128)S(1)}, u32[]{:S(2)}, u32[]{:S(2)}) %collective-permute-start.41) | collective-permute-done | bytes 1088 | tf_op jit(solution)/shard_map/ppermute | solution.py:32
  (315 shorter events, 135.7 us)
Async XLA Ops:
  0.7 12.3 %collective-permute-start.7 = (f32[1,1,64,512]{3,2,1,0:T(8,128)S(1)}, f32[1,1,64,512]{3,2,1,0:T(8,128)S(1)}, u32[]{:S(2)}, u32[]{:S(2)}) collective-permute-start(f32[1,1,64,512]{3,2,1,0:T(8,128)S(1)} %broadcast.185), channel_id=1, source_target_pairs={{8,0},{16,8},{24,16},{9,1},{17,9},{25,17},{10,2},{18,10},{26,18},{... | collective-permute-start | bytes 393224 | tf_op jit(solution)/shard_map/ppermute | solution.py:32
  2.7 10.3 %collective-permute-start.6 = (f32[1,1,64,512]{3,2,1,0:T(8,128)S(1)}, f32[1,1,64,512]{3,2,1,0:T(8,128)S(1)}, u32[]{:S(2)}, u32[]{:S(2)}) collective-permute-start(f32[1,1,64,512]{3,2,1,0:T(8,128)S(1)} %broadcast.185), channel_id=1, source_target_pairs={{0,8},{8,16},{16,24},{1,9},{9,17},{17,25},{2,10},{10,18},{18,26},{... | collective-permute-start | bytes 393224 | tf_op jit(solution)/shard_map/ppermute | solution.py:30
  7.2 10.6 %collective-permute-start = (f32[2,1,64,512]{3,2,1,0:T(8,128)S(1)}, f32[2,1,64,512]{3,2,1,0:T(8,128)S(1)}, u32[]{:S(2)}, u32[]{:S(2)}) collective-permute-start(f32[2,1,64,512]{3,2,1,0:T(8,128)S(1)} %get-tuple-element.40), channel_id=1, source_target_pairs={{0,8},{8,16},{16,24},{1,9},{9,17},{17,25},{2,10},{10,18},{18,26},{... | collective-permute-start | bytes 786440 | tf_op jit(solution)/shard_map/ppermute | solution.py:30
  9.2 8.7 %collective-permute-start.1 = (f32[2,1,64,512]{3,2,1,0:T(8,128)S(1)}, f32[2,1,64,512]{3,2,1,0:T(8,128)S(1)}, u32[]{:S(2)}, u32[]{:S(2)}) collective-permute-start(f32[2,1,64,512]{3,2,1,0:T(8,128)S(1)} %get-tuple-element.41), channel_id=1, source_target_pairs={{8,0},{16,8},{24,16},{9,1},{17,9},{25,17},{10,2},{18,10},{26,18},{... | collective-permute-start | bytes 786440 | tf_op jit(solution)/shard_map/ppermute | solution.py:32
  13.1 10.7 %collective-permute-start.8 = (f32[1,4,1,512]{3,2,1,0:T(1,128)S(1)}, f32[1,4,1,512]{3,2,1,0:T(1,128)S(1)}, u32[]{:S(2)}, u32[]{:S(2)}) collective-permute-start(f32[1,4,1,512]{3,2,1,0:T(1,128)S(1)} %get-tuple-element.42), channel_id=1, source_target_pairs={{0,2},{2,4},{4,6},{1,3},{3,5},{5,7},{8,10},{10,12},{12,14},{9,11},... | collective-permute-start | bytes 24584 | tf_op jit(solution)/shard_map/ppermute | solution.py:30
  16.5 7.2 %collective-permute-start.9 = (f32[1,4,1,512]{3,2,1,0:T(1,128)S(1)}, f32[1,4,1,512]{3,2,1,0:T(1,128)S(1)}, u32[]{:S(2)}, u32[]{:S(2)}) collective-permute-start(f32[1,4,1,512]{3,2,1,0:T(1,128)S(1)} %get-tuple-element.43), channel_id=1, source_target_pairs={{2,0},{4,2},{6,4},{3,1},{5,3},{7,5},{10,8},{12,10},{14,12},{11,9},... | collective-permute-start | bytes 24584 | tf_op jit(solution)/shard_map/ppermute | solution.py:32
  17.9 10.7 %collective-permute-start.2 = (f32[2,4,1,512]{3,2,1,0:T(1,128)S(1)}, f32[2,4,1,512]{3,2,1,0:T(1,128)S(1)}, u32[]{:S(2)}, u32[]{:S(2)}) collective-permute-start(f32[2,4,1,512]{3,2,1,0:T(1,128)S(1)} %get-tuple-element.16), channel_id=1, source_target_pairs={{0,2},{2,4},{4,6},{1,3},{3,5},{5,7},{8,10},{10,12},{12,14},{9,11},... | collective-permute-start | bytes 49160 | tf_op jit(solution)/shard_map/ppermute | solution.py:30
  22.5 6.2 %collective-permute-start.3 = (f32[2,4,1,512]{3,2,1,0:T(1,128)S(1)}, f32[2,4,1,512]{3,2,1,0:T(1,128)S(1)}, u32[]{:S(2)}, u32[]{:S(2)}) collective-permute-start(f32[2,4,1,512]{3,2,1,0:T(1,128)S(1)} %get-tuple-element.17), channel_id=1, source_target_pairs={{2,0},{4,2},{6,4},{3,1},{5,3},{7,5},{10,8},{12,10},{14,12},{11,9},... | collective-permute-start | bytes 49160 | tf_op jit(solution)/shard_map/ppermute | solution.py:32
  23.9 10.8 %collective-permute-start.10 = (f32[1,4,66,1]{3,2,1,0:T(8,128)S(1)}, f32[1,4,66,1]{3,2,1,0:T(8,128)S(1)}, u32[]{:S(2)}, u32[]{:S(2)}) collective-permute-start(f32[1,4,66,1]{3,2,1,0:T(8,128)S(1)} %get-tuple-element.28), channel_id=1, source_target_pairs={{0,1},{2,3},{4,5},{6,7},{8,9},{10,11},{12,13},{14,15},{16,17},{18,... | collective-permute-start | bytes 3176 | tf_op jit(solution)/shard_map/ppermute | solution.py:30
  27.4 7.4 %collective-permute-start.11 = (f32[1,4,66,1]{3,2,1,0:T(8,128)S(1)}, f32[1,4,66,1]{3,2,1,0:T(8,128)S(1)}, u32[]{:S(2)}, u32[]{:S(2)}) collective-permute-start(f32[1,4,66,1]{3,2,1,0:T(8,128)S(1)} %get-tuple-element.29), channel_id=1, source_target_pairs={{1,0},{3,2},{5,4},{7,6},{9,8},{11,10},{13,12},{15,14},{17,16},{19,... | collective-permute-start | bytes 3176 | tf_op jit(solution)/shard_map/ppermute | solution.py:32
  28.8 8.8 %collective-permute-start.4 = (f32[2,4,66,1]{3,2,1,0:T(8,128)S(1)}, f32[2,4,66,1]{3,2,1,0:T(8,128)S(1)}, u32[]{:S(2)}, u32[]{:S(2)}) collective-permute-start(f32[2,4,66,1]{3,2,1,0:T(8,128)S(1)} %get-tuple-element.14), channel_id=1, source_target_pairs={{0,1},{2,3},{4,5},{6,7},{8,9},{10,11},{12,13},{14,15},{16,17},{18,... | collective-permute-start | bytes 6344 | tf_op jit(solution)/shard_map/ppermute | solution.py:30
  33.4 8.6 %collective-permute-start.5 = (f32[2,4,66,1]{3,2,1,0:T(8,128)S(1)}, f32[2,4,66,1]{3,2,1,0:T(8,128)S(1)}, u32[]{:S(2)}, u32[]{:S(2)}) collective-permute-start(f32[2,4,66,1]{3,2,1,0:T(8,128)S(1)} %get-tuple-element.15), channel_id=1, source_target_pairs={{1,0},{3,2},{5,4},{7,6},{9,8},{11,10},{13,12},{15,14},{17,16},{19,... | collective-permute-start | bytes 6344 | tf_op jit(solution)/shard_map/ppermute | solution.py:32
  145.0 7.7 %collective-permute-start.12 = (f32[1,1,64,512]{3,2,1,0:T(8,128)S(1)}, f32[1,1,64,512]{3,2,1,0:T(8,128)S(1)}, u32[]{:S(2)}, u32[]{:S(2)}) collective-permute-start(f32[1,1,64,512]{3,2,1,0:T(8,128)S(1)} %get-tuple-element.52), channel_id=1, source_target_pairs={{0,8},{8,16},{16,24},{1,9},{9,17},{17,25},{2,10},{10,18},{18,26},{... | collective-permute-start | bytes 393224 | tf_op jit(solution)/shard_map/ppermute | solution.py:30
  146.9 6.1 %collective-permute-start.13 = (f32[1,1,64,512]{3,2,1,0:T(8,128)S(1)}, f32[1,1,64,512]{3,2,1,0:T(8,128)S(1)}, u32[]{:S(2)}, u32[]{:S(2)}) collective-permute-start(f32[1,1,64,512]{3,2,1,0:T(8,128)S(1)} %get-tuple-element.53), channel_id=1, source_target_pairs={{8,0},{16,8},{24,16},{9,1},{17,9},{25,17},{10,2},{18,10},{26,18},{... | collective-permute-start | bytes 393224 | tf_op jit(solution)/shard_map/ppermute | solution.py:32
  154.4 5.5 %collective-permute-start.15 = (f32[1,4,1,512]{3,2,1,0:T(1,128)S(1)}, f32[1,4,1,512]{3,2,1,0:T(1,128)S(1)}, u32[]{:S(2)}, u32[]{:S(2)}) collective-permute-start(f32[1,4,1,512]{3,2,1,0:T(1,128)S(1)} %get-tuple-element.39), channel_id=1, source_target_pairs={{2,0},{4,2},{6,4},{3,1},{5,3},{7,5},{10,8},{12,10},{14,12},{11,9},... | collective-permute-start | bytes 24584 | tf_op jit(solution)/shard_map/ppermute | solution.py:32
  160.7 11.1 %collective-permute-start.16 = (f32[1,4,66,1]{3,2,1,0:T(8,128)}, f32[1,4,66,1]{3,2,1,0:T(8,128)S(1)}, u32[]{:S(2)}, u32[]{:S(2)}) collective-permute-start(f32[1,4,66,1]{3,2,1,0:T(8,128)} %get-tuple-element.26), channel_id=1, source_target_pairs={{0,1},{2,3},{4,5},{6,7},{8,9},{10,11},{12,13},{14,15},{16,17},{18,... | collective-permute-start | bytes 3176 | tf_op jit(solution)/shard_map/ppermute | solution.py:30
  162.9 10.2 %collective-permute-start.17 = (f32[1,4,66,1]{3,2,1,0:T(8,128)}, f32[1,4,66,1]{3,2,1,0:T(8,128)}, u32[]{:S(2)}, u32[]{:S(2)}) collective-permute-start(f32[1,4,66,1]{3,2,1,0:T(8,128)} %get-tuple-element.27), channel_id=1, source_target_pairs={{1,0},{3,2},{5,4},{7,6},{9,8},{11,10},{13,12},{15,14},{17,16},{19,... | collective-permute-start | bytes 3176 | tf_op jit(solution)/shard_map/ppermute | solution.py:32
  177.7 11.1 %collective-permute-start.18 = (f32[1,1,64,512]{3,2,1,0:T(8,128)}, f32[1,1,64,512]{3,2,1,0:T(8,128)}, u32[]{:S(2)}, u32[]{:S(2)}) collective-permute-start(f32[1,1,64,512]{3,2,1,0:T(8,128)} %get-tuple-element.50), channel_id=1, source_target_pairs={{0,8},{8,16},{16,24},{1,9},{9,17},{17,25},{2,10},{10,18},{18,26},{... | collective-permute-start | bytes 393224 | tf_op jit(solution)/shard_map/ppermute | solution.py:30
  179.6 9.2 %collective-permute-start.19 = (f32[1,1,64,512]{3,2,1,0:T(8,128)}, f32[1,1,64,512]{3,2,1,0:T(8,128)}, u32[]{:S(2)}, u32[]{:S(2)}) collective-permute-start(f32[1,1,64,512]{3,2,1,0:T(8,128)} %get-tuple-element.51), channel_id=1, source_target_pairs={{8,0},{16,8},{24,16},{9,1},{17,9},{25,17},{10,2},{18,10},{26,18},{... | collective-permute-start | bytes 393224 | tf_op jit(solution)/shard_map/ppermute | solution.py:32
  197.9 7.5 %collective-permute-start.22 = (f32[1,4,66,1]{3,2,1,0:T(8,128)S(1)}, f32[1,4,66,1]{3,2,1,0:T(8,128)S(1)}, u32[]{:S(2)}, u32[]{:S(2)}) collective-permute-start(f32[1,4,66,1]{3,2,1,0:T(8,128)S(1)} %get-tuple-element.24), channel_id=1, source_target_pairs={{0,1},{2,3},{4,5},{6,7},{8,9},{10,11},{12,13},{14,15},{16,17},{18,... | collective-permute-start | bytes 3176 | tf_op jit(solution)/shard_map/ppermute | solution.py:30
  201.9 7.0 %collective-permute-start.23 = (f32[1,4,66,1]{3,2,1,0:T(8,128)S(1)}, f32[1,4,66,1]{3,2,1,0:T(8,128)S(1)}, u32[]{:S(2)}, u32[]{:S(2)}) collective-permute-start(f32[1,4,66,1]{3,2,1,0:T(8,128)S(1)} %get-tuple-element.25), channel_id=1, source_target_pairs={{1,0},{3,2},{5,4},{7,6},{9,8},{11,10},{13,12},{15,14},{17,16},{19,... | collective-permute-start | bytes 3176 | tf_op jit(solution)/shard_map/ppermute | solution.py:32
  211.3 6.4 %collective-permute-start.24 = (f32[1,1,64,512]{3,2,1,0:T(8,128)S(1)}, f32[1,1,64,512]{3,2,1,0:T(8,128)S(1)}, u32[]{:S(2)}, u32[]{:S(2)}) collective-permute-start(f32[1,1,64,512]{3,2,1,0:T(8,128)S(1)} %get-tuple-element.48), channel_id=1, source_target_pairs={{0,8},{8,16},{16,24},{1,9},{9,17},{17,25},{2,10},{10,18},{18,26},{... | collective-permute-start | bytes 393224 | tf_op jit(solution)/shard_map/ppermute | solution.py:30
  213.3 6.1 %collective-permute-start.25 = (f32[1,1,64,512]{3,2,1,0:T(8,128)S(1)}, f32[1,1,64,512]{3,2,1,0:T(8,128)S(1)}, u32[]{:S(2)}, u32[]{:S(2)}) collective-permute-start(f32[1,1,64,512]{3,2,1,0:T(8,128)S(1)} %get-tuple-element.49), channel_id=1, source_target_pairs={{8,0},{16,8},{24,16},{9,1},{17,9},{25,17},{10,2},{18,10},{26,18},{... | collective-permute-start | bytes 393224 | tf_op jit(solution)/shard_map/ppermute | solution.py:32
  228.6 7.0 %collective-permute-start.29 = (f32[1,4,66,1]{3,2,1,0:T(8,128)S(1)}, f32[1,4,66,1]{3,2,1,0:T(8,128)S(1)}, u32[]{:S(2)}, u32[]{:S(2)}) collective-permute-start(f32[1,4,66,1]{3,2,1,0:T(8,128)S(1)} %get-tuple-element.23), channel_id=1, source_target_pairs={{1,0},{3,2},{5,4},{7,6},{9,8},{11,10},{13,12},{15,14},{17,16},{19,... | collective-permute-start | bytes 3176 | tf_op jit(solution)/shard_map/ppermute | solution.py:32
  334.8 7.7 %collective-permute-start.30 = (f32[1,1,64,512]{3,2,1,0:T(8,128)S(1)}, f32[1,1,64,512]{3,2,1,0:T(8,128)S(1)}, u32[]{:S(2)}, u32[]{:S(2)}) collective-permute-start(f32[1,1,64,512]{3,2,1,0:T(8,128)S(1)} %get-tuple-element.46), channel_id=1, source_target_pairs={{0,8},{8,16},{16,24},{1,9},{9,17},{17,25},{2,10},{10,18},{18,26},{... | collective-permute-start | bytes 393224 | tf_op jit(solution)/shard_map/ppermute | solution.py:30
  336.8 6.1 %collective-permute-start.31 = (f32[1,1,64,512]{3,2,1,0:T(8,128)S(1)}, f32[1,1,64,512]{3,2,1,0:T(8,128)S(1)}, u32[]{:S(2)}, u32[]{:S(2)}) collective-permute-start(f32[1,1,64,512]{3,2,1,0:T(8,128)S(1)} %get-tuple-element.47), channel_id=1, source_target_pairs={{8,0},{16,8},{24,16},{9,1},{17,9},{25,17},{10,2},{18,10},{26,18},{... | collective-permute-start | bytes 393224 | tf_op jit(solution)/shard_map/ppermute | solution.py:32
  350.6 11.7 %collective-permute-start.34 = (f32[1,4,66,1]{3,2,1,0:T(8,128)}, f32[1,4,66,1]{3,2,1,0:T(8,128)S(1)}, u32[]{:S(2)}, u32[]{:S(2)}) collective-permute-start(f32[1,4,66,1]{3,2,1,0:T(8,128)} %get-tuple-element.20), channel_id=1, source_target_pairs={{0,1},{2,3},{4,5},{6,7},{8,9},{10,11},{12,13},{14,15},{16,17},{18,... | collective-permute-start | bytes 3176 | tf_op jit(solution)/shard_map/ppermute | solution.py:30
  354.5 8.9 %collective-permute-start.35 = (f32[1,4,66,1]{3,2,1,0:T(8,128)}, f32[1,4,66,1]{3,2,1,0:T(8,128)}, u32[]{:S(2)}, u32[]{:S(2)}) collective-permute-start(f32[1,4,66,1]{3,2,1,0:T(8,128)} %get-tuple-element.21), channel_id=1, source_target_pairs={{1,0},{3,2},{5,4},{7,6},{9,8},{11,10},{13,12},{15,14},{17,16},{19,... | collective-permute-start | bytes 3176 | tf_op jit(solution)/shard_map/ppermute | solution.py:32
  367.4 11.2 %collective-permute-start.36 = (f32[1,1,64,512]{3,2,1,0:T(8,128)}, f32[1,1,64,512]{3,2,1,0:T(8,128)}, u32[]{:S(2)}, u32[]{:S(2)}) collective-permute-start(f32[1,1,64,512]{3,2,1,0:T(8,128)} %get-tuple-element.44), channel_id=1, source_target_pairs={{0,8},{8,16},{16,24},{1,9},{9,17},{17,25},{2,10},{10,18},{18,26},{... | collective-permute-start | bytes 393224 | tf_op jit(solution)/shard_map/ppermute | solution.py:30
  369.3 9.3 %collective-permute-start.37 = (f32[1,1,64,512]{3,2,1,0:T(8,128)}, f32[1,1,64,512]{3,2,1,0:T(8,128)}, u32[]{:S(2)}, u32[]{:S(2)}) collective-permute-start(f32[1,1,64,512]{3,2,1,0:T(8,128)} %get-tuple-element.45), channel_id=1, source_target_pairs={{8,0},{16,8},{24,16},{9,1},{17,9},{25,17},{10,2},{18,10},{26,18},{... | collective-permute-start | bytes 393224 | tf_op jit(solution)/shard_map/ppermute | solution.py:32
  387.6 6.6 %collective-permute-start.40 = (f32[1,4,66,1]{3,2,1,0:T(8,128)S(1)}, f32[1,4,66,1]{3,2,1,0:T(8,128)S(1)}, u32[]{:S(2)}, u32[]{:S(2)}) collective-permute-start(f32[1,4,66,1]{3,2,1,0:T(8,128)S(1)} %get-tuple-element.18), channel_id=1, source_target_pairs={{0,1},{2,3},{4,5},{6,7},{8,9},{10,11},{12,13},{14,15},{16,17},{18,... | collective-permute-start | bytes 3176 | tf_op jit(solution)/shard_map/ppermute | solution.py:30
  391.5 7.0 %collective-permute-start.41 = (f32[1,4,66,1]{3,2,1,0:T(8,128)S(1)}, f32[1,4,66,1]{3,2,1,0:T(8,128)S(1)}, u32[]{:S(2)}, u32[]{:S(2)}) collective-permute-start(f32[1,4,66,1]{3,2,1,0:T(8,128)S(1)} %get-tuple-element.19), channel_id=1, source_target_pairs={{1,0},{3,2},{5,4},{7,6},{9,8},{11,10},{13,12},{15,14},{17,16},{19,... | collective-permute-start | bytes 3176 | tf_op jit(solution)/shard_map/ppermute | solution.py:32
  (73 other events, 1191.1 us)
